TPU v7x, 32 devices: a whole 2x2x4 slice. The times are simulated.
32 devices in a mesh: rep: 16 (over z, y, core), zero: 2 (over x).
Axes of the slice: x: 2, y: 2, z: 4, core: 2. Of those that a mesh axis runs over, the one named last changes fastest.
Arguments:
- tokens: bfloat16 [8192, 1536], P(('rep', 'zero')), may hold values from -6 to 6
- cotangent: bfloat16 [8192, 1536], P(('rep', 'zero')), may hold values from -6 to 6
- segment_ids: int32 [8192], P(('rep', 'zero')), may hold values from 0 to 52, never falling along the last dimension, each value on 1 to 512 neighbouring positions
- master: float32 [14647296], P('zero')
- first_moment: float32 [14647296], P('zero')
- second_moment: float32 [14647296], P('zero')
- step_count: int32 [], replicated, may hold values from 1 to 20
- rates: float32 [2, 9], replicated, may hold values from 0 to 1
Outputs:
- mixed: bfloat16 [8192, 1536], P(('rep', 'zero'))
- input_grad: bfloat16 [8192, 1536], P(('rep', 'zero'))
- new_first: float32 [14647296], P('zero')
- new_second: float32 [14647296], P('zero')
- new_master: float32 [14647296], P('zero')
Inputs may be any that keep to these rules, and one draw needn't show every extreme that they name: `segment_ids`: ids never fall along the tokens; a document is a run of equal ids of at most 512 tokens.
All inputs are finite; a program needn't handle non-finite values.
Results may differ from a plain program's by a relative error of at most 0.012.
Values may be sent and summed in bfloat16 or wider, within the bound.
No kernel may reach another device: no remote copies, remote signals or barrier semaphores. Data moves between devices by JAX's collectives and lax.ppermute only.
A program may use at most 512 MiB of HBM per device.

v0:
```python
import functools
import jax
import jax.numpy as jnp
from jax import lax
from jax.sharding import PartitionSpec as P

D = 1536
DI = 3072
NS = 128
HD = 64
NH = 48
E = 6448
CONV = 3328
EPSILON = 1e-05
ADAM_EPSILON = 1e-08
BETA_ONE = 0.5
BETA_TWO = 0.5
HEAD_GROUP = 4
HIGHEST = lax.Precision.HIGHEST


def piece_bounds():
    amounts = [D * E, DI * D, 4 * CONV, CONV, D, DI, NH, NH, NH]
    bounds = [0]
    for amount in amounts:
        bounds.append(bounds[-1] + amount)
    return bounds


def unpack(flat_values):
    bounds = piece_bounds()
    shapes = [(D, E), (DI, D), (4, CONV), (CONV,), (D,), (DI,), (NH,), (NH,), (NH,)]
    return tuple(
        (
            flat_values[bounds[piece_index] : bounds[piece_index + 1]].reshape(shapes[piece_index])
            for piece_index in range(9)
        )
    )


def contract(left, right, left_dim, right_dim):
    return lax.dot_general(
        left, right, (((left_dim,), (right_dim,)), ((), ())), preferred_element_type=jnp.float32
    )


def prenorm(residual, norm_gain):
    inverse_rms = lax.rsqrt(jnp.mean(residual * residual, axis=-1, keepdims=True) + EPSILON)
    return residual * inverse_rms * norm_gain


def head_group(contact, allowed, inputs):
    group_decay, group_step, group_values = inputs
    log_gap = group_decay[:, :, None] - group_decay[:, None, :]
    kernel = (
        jnp.exp(jnp.where(allowed[None], log_gap, -1e30)) * contact[None] * group_step[:, None, :]
    )
    return jnp.einsum("gts,gsp->gtp", kernel, group_values, precision=HIGHEST)


def mixer(
    segment_ids, projected, filter_taps, filter_bias, step_bias, log_decay, skip_weight, gate_gain
):
    length = projected.shape[0]
    gate_raw = projected[:, :DI]
    filter_in = projected[:, DI : DI + CONV]
    step_raw = projected[:, DI + CONV :]
    padded = jnp.pad(filter_in, ((3, 0), (0, 0)))
    padded_ids = jnp.pad(segment_ids, (3, 0), constant_values=-1)
    filtered = jnp.zeros_like(filter_in) + filter_bias[None, :]
    for offset in range(4):
        same_segment = (padded_ids[offset : offset + length] == segment_ids)[:, None]
        filtered = filtered + jnp.where(
            same_segment, padded[offset : offset + length] * filter_taps[offset][None, :], 0.0
        )
    activated = jax.nn.silu(filtered)
    values = activated[:, :DI].reshape(length, NH, HD)
    b_input = activated[:, DI : DI + NS]
    c_output = activated[:, DI + NS :]
    step_size = jax.nn.softplus(step_raw + step_bias[None, :])
    cumulative = jnp.cumsum(step_size * (-jnp.exp(log_decay))[None, :], axis=0)
    row_index = lax.broadcasted_iota(jnp.int32, (length, length), 0)
    col_index = lax.broadcasted_iota(jnp.int32, (length, length), 1)
    allowed = (col_index <= row_index) & (segment_ids[:, None] == segment_ids[None, :])
    contact = lax.dot_general(c_output, b_input, (((1,), (1,)), ((), ())), precision=HIGHEST)
    groups = NH // HEAD_GROUP
    grouped_decay = cumulative.T.reshape(groups, HEAD_GROUP, length)
    grouped_step = step_size.T.reshape(groups, HEAD_GROUP, length)
    grouped_values = values.transpose(1, 0, 2).reshape(groups, HEAD_GROUP, length, HD)
    scanned = lax.map(
        jax.checkpoint(functools.partial(head_group, contact, allowed)),
        (grouped_decay, grouped_step, grouped_values),
    )
    ssd_out = (
        scanned.reshape(NH, length, HD).transpose(1, 0, 2) + skip_weight[None, :, None] * values
    )
    gated = ssd_out.reshape(length, DI) * jax.nn.silu(gate_raw)
    inverse_rms = lax.rsqrt(jnp.mean(gated * gated, axis=-1, keepdims=True) + EPSILON)
    return gated * inverse_rms * gate_gain


def adamw(gradient, first_moment, second_moment, weights, start, step_count, rates):
    position = start + lax.iota(jnp.int32, gradient.shape[0])
    bounds = piece_bounds()
    learn_rate = jnp.zeros_like(gradient)
    decay_rate = jnp.zeros_like(gradient)
    for piece_index in range(9):
        inside = (position >= bounds[piece_index]) & (position < bounds[piece_index + 1])
        learn_rate = learn_rate + jnp.where(inside, rates[0, piece_index], 0.0)
        decay_rate = decay_rate + jnp.where(inside, rates[1, piece_index], 0.0)
    new_first = BETA_ONE * first_moment + (1.0 - BETA_ONE) * gradient
    new_second = BETA_TWO * second_moment + (1.0 - BETA_TWO) * gradient * gradient
    power = step_count.astype(gradient.dtype)
    correct_one = 1.0 - jnp.power(BETA_ONE, power)
    correct_two = 1.0 - jnp.power(BETA_TWO, power)
    update = (
        new_first / correct_one / (jnp.sqrt(new_second / correct_two) + ADAM_EPSILON)
        + decay_rate * weights
    )
    return (new_first, new_second, weights - learn_rate * update)


def gather_weights(master):
    rep_size = lax.axis_size("rep")
    zero_size = lax.axis_size("zero")
    shard_size = master.shape[0]
    piece_size = shard_size // rep_size
    rep_index = lax.axis_index("rep")
    zero_index = lax.axis_index("zero")
    own = master.astype(jnp.bfloat16)
    mine = lax.dynamic_slice_in_dim(own, rep_index * piece_size, piece_size)
    if zero_size == 2:
        other_piece = lax.ppermute(mine, "zero", [(0, 1), (1, 0)])
        other = lax.all_gather(other_piece, "rep", axis=0, tiled=True)
        shards = [jnp.where(zero_index == 0, own, other), jnp.where(zero_index == 0, other, own)]
    else:
        across = lax.all_gather(mine, "zero", axis=0, tiled=True)
        shards = [
            lax.all_gather(
                lax.dynamic_slice_in_dim(across, shard * piece_size, piece_size),
                "rep",
                axis=0,
                tiled=True,
            )
            for shard in range(zero_size)
        ]
    return jnp.concatenate(shards)


def reduce_gradient(pieces, shard_size):
    zero_size = lax.axis_size("zero")
    total_params = shard_size * zero_size
    flat_grad = jnp.zeros((total_params,), jnp.bfloat16)
    offset = 0
    for piece_grad in pieces:
        flat_piece = piece_grad.reshape(-1).astype(jnp.bfloat16)
        flat_grad = lax.dynamic_update_slice_in_dim(flat_grad, flat_piece, offset, 0)
        offset += flat_piece.shape[0]
    summed = lax.psum(flat_grad, ("rep", "zero"))
    return lax.dynamic_slice_in_dim(summed, lax.axis_index("zero") * shard_size, shard_size)


def body(tokens, cotangent, segment_ids, master, first_moment, second_moment, step_count, rates):
    gathered = gather_weights(master)
    (
        in_projection,
        out_projection,
        filter_taps,
        filter_bias,
        norm_gain,
        gate_gain,
        step_bias,
        log_decay,
        skip_weight,
    ) = unpack(gathered)
    residual = tokens.astype(jnp.float32)
    normed, norm_pullback = jax.vjp(prenorm, residual, norm_gain.astype(jnp.float32))
    normed_low = normed.astype(jnp.bfloat16)
    projected = jnp.dot(normed_low, in_projection, preferred_element_type=jnp.float32)
    mixer_out, mixer_pullback = jax.vjp(
        functools.partial(mixer, segment_ids),
        projected,
        filter_taps.astype(jnp.float32),
        filter_bias.astype(jnp.float32),
        step_bias.astype(jnp.float32),
        log_decay.astype(jnp.float32),
        skip_weight.astype(jnp.float32),
        gate_gain.astype(jnp.float32),
    )
    mixer_low = mixer_out.astype(jnp.bfloat16)
    branch = jnp.dot(mixer_low, out_projection, preferred_element_type=jnp.float32)
    mixed = (residual + branch).astype(jnp.bfloat16)
    grad_out = contract(mixer_low, cotangent, 0, 0)
    grad_mixer = contract(cotangent, out_projection, 1, 1)
    grad_projected, grad_taps, grad_bias, grad_step_bias, grad_decay, grad_skip, grad_gate_gain = (
        mixer_pullback(grad_mixer)
    )
    projected_low = grad_projected.astype(jnp.bfloat16)
    grad_in = contract(normed_low, projected_low, 0, 0)
    grad_normed = contract(projected_low, in_projection, 1, 1)
    grad_residual, grad_norm_gain = norm_pullback(grad_normed)
    input_grad = (cotangent.astype(jnp.float32) + grad_residual).astype(jnp.bfloat16)
    pieces = [
        grad_in,
        grad_out,
        grad_taps,
        grad_bias,
        grad_norm_gain,
        grad_gate_gain,
        grad_step_bias,
        grad_decay,
        grad_skip,
    ]
    shard_size = master.shape[0]
    gradient = reduce_gradient(pieces, shard_size).astype(jnp.float32)
    shard_start = lax.axis_index("zero") * shard_size
    new_first, new_second, new_master = adamw(
        gradient, first_moment, second_moment, master, shard_start, step_count, rates
    )
    return (mixed, input_grad, new_first, new_second, new_master)


def solution(mesh):
    in_specs = (
        P(("rep", "zero"), None),
        P(("rep", "zero"), None),
        P(("rep", "zero")),
        P("zero"),
        P("zero"),
        P("zero"),
        P(),
        P(),
    )
    out_specs = (
        P(("rep", "zero"), None),
        P(("rep", "zero"), None),
        P("zero"),
        P("zero"),
        P("zero"),
    )
    return jax.shard_map(body, mesh=mesh, in_specs=in_specs, out_specs=out_specs, check_vma=False)
```

profile of v0, /device:TPU:0, one launch (start us, length us, event | category | flops | bytes accessed | tf_op | source)
XLA Modules:
  0.0 1149.5 jit_solution(654857939169219657)
XLA Ops:
  7.2 16.2 %convert_element_type.91 = bf16[7323648]{0:T(1024)(128)(2,1)} convert(f32[7323648]{0:T(1024)} %param.15) | non-fusion elementwise | flops 7323648 | bytes 43941888 | tf_op jit(solution)/shard_map/convert_element_type | solution.py:130
  24.7 3.0 collective-permute-start
  27.7 20.3 %collective-permute-done = bf16[457728]{0:T(1024)(128)(2,1)S(1)} collective-permute-done((bf16[457728]{0:T(1024)(128)(2,1)S(1)}, bf16[457728]{0:T(1024)(128)(2,1)S(1)}, u32[]{:S(2)}, u32[]{:S(2)}) %collective-permute-start) | collective-permute-done | bytes 915488 | tf_op jit(solution)/shard_map/ppermute | solution.py:133
  50.1 113.6 %all-gather.2.cloned.1.call-done = bf16[7323648]{0:T(1024)(128)(2,1)} async-done(((bf16[457728]{0:T(1024)(128)(2,1)}), bf16[7323648]{0:T(1024)(128)(2,1)}) %all-gather.2.cloned.1.call-update) | async-done | bytes 14647312 | tf_op jit(solution)/shard_map/all_gather | solution.py:134
  163.8 25.1 %broadcast_select_fusion = (bf16[7323648]{0:T(1024)(128)(2,1)}, bf16[7323648]{0:T(1024)(128)(2,1)}) fusion(bf16[7323648]{0:T(1024)(128)(2,1)} %all-gather.2.cloned.1.call-done, pred[]{:T(512)S(6)} %eq.39, f32[7323648]{0:T(1024)} %param.15), kind=kLoop, calls=%fused_computation.81 | loop fusion | flops 21970944 | bytes 73236480 | tf_op jit(solution)/shard_map/jit(_where)/select_n | solution.py:135
  194.4 20.2 %pad_maximum_fusion = bf16[9904128]{0:T(1024)(128)(2,1)} fusion(bf16[7323648]{0:T(1024)(128)(2,1)} %get-tuple-element.429, bf16[7323648]{0:T(1024)(128)(2,1)} %get-tuple-element.428), kind=kLoop, calls=%fused_computation.80 | loop fusion | flops 39616512 | bytes 49102848 | tf_op jit(solution)/shard_map/concatenate | solution.py:147
  214.6 32.9 %reshape.260 = bf16[1536,6448]{1,0:T(8,128)(2,1)} reshape(bf16[9904128]{0:T(1024)(128)(2,1)} %pad_maximum_fusion) | data formatting | bytes 39616512 | tf_op jit(solution)/shard_map/reshape | solution.py:35
  247.5 13.0 %fusion.80 = f32[256,6448]{0,1:T(8,128)S(1)} fusion(bf16[1536,6448]{1,0:T(8,128)(2,1)} %reshape.260, bf16[256,1536]{1,0:T(8,128)(2,1)} %param.12, f32[1536]{0:T(1024)S(1)} %slice_convert_fusion.3, f32[256]{0:T(256)S(1)} %fusion.99), kind=kOutput, calls=%fused_computation.139 | convolution fusion | flops 5072486400 | bytes 27204608 | tf_op jit(solution)/shard_map/dot_general | solution.py:179
  260.8 7.5 fusion.64
  271.7 9.1 slice.224
  282.3 30.5 %while.33 = (s32[]{:T(128)}, f32[12,4,256,64]{2,3,1,0:T(8,128)S(1)}, f32[12,4,256]{2,1,0:T(4,128)S(1)}, f32[1,256,256]{2,1,0:T(8,128)}, f32[12,4,256]{2,1,0:T(4,...) while((s32[]{:T(128)}, f32[12,4,256,64]{2,3,1,0:T(8,128)S(1)}, ...), condition=%wide.region_4.5_spmd.clone, body=%wide.region_3.4_spmd.clone.sunk | while | flops 202375168 | bytes 881761 | solution.py:90
  315.5 4.1 multiply_reduce_fusion.9
  319.6 18.0 %slice.185 = bf16[3072,1536]{1,0:T(8,128)(2,1)} reshape(bf16[4718592]{0:T(1024)(128)(2,1)} %slice.224) | data formatting | bytes 18874368 | tf_op jit(solution)/shard_map/slice | solution.py:35
  337.6 6.8 convolution_convert_fusion.1
  344.4 3.8 multiply_reduce_fusion.7
  348.2 6.7 multiply_reduce_fusion.6
  357.0 78.3 %while.34 = (s32[]{:T(128)}, f32[256,256]{1,0:T(8,128)S(1)}, f32[12,4,256]{2,1,0:T(4,128)S(1)}, f32[12,4,256]{2,1,0:T(4,128)S(1)}, f32[12,4,256,64]{2,3,1,0:T(8,...) while((s32[]{:T(128)}, f32[256,256]{1,0:T(8,128)S(1)}, ...), condition=%wide.region_12.13_spmd.clone, body=%wide.region_7.12_spmd.clone.sunk | while | flops 407370752 | bytes 4986067 | solution.py:90
  443.1 5.0 bitcast_add_fusion
  449.0 8.4 multiply_reduce_fusion.4
  457.5 3.6 broadcast_multiply_fusion
  462.1 6.8 pad_add_fusion
  468.9 13.1 %fusion.72 = (bf16[1536]{0:T(1024)(128)(2,1)S(1)}, f32[256]{0:T(256)S(1)}, f32[256,1536]{1,0:T(8,128)}) fusion(bf16[256,1536]{1,0:T(8,128)(2,1)} %param.12, f32[256]{0:T(256)S(1)} %copy-done.46, f32[1536]{0:T(1024)S(1)} %slice_convert_fusion.3, bf16[1536,6448]{1,0:T(8,128)(2,1)} %reshape.260, f32[256,3072]{0,1:T(8,128)} %get-tuple-element.432, ...), kind=kOutput, calls=%fused_computation.131 | convolution fusion | flops 5078616064 | bytes 28781568 | tf_op jit(solution)/shard_map/dot_general | solution.py:42
  482.0 13.1 %convolution_convert_fusion = bf16[1536,6448]{0,1:T(8,128)(2,1)} fusion(bf16[256,1536]{1,0:T(8,128)(2,1)} %param.12, f32[1536]{0:T(1024)S(1)} %slice_convert_fusion.3, f32[256]{0:T(256)S(1)} %copy-done.46, f32[256,3072]{0,1:T(8,128)} %get-tuple-element.432, f32[256,3328]{0,1:T(8,128)} %pad_add_fusion, f32[256,48]{0,1:T(8,128)S(1)} %get-tuple-element.416), kind=kOutput, calls=%fused_computation.79 | convolution fusion | flops 5087342592 | bytes 27204608 | tf_op jit(solution)/shard_map/dot_general | solution.py:42
  495.1 18.1 %convert_element_type.108 = bf16[4718592]{0:T(1024)(128)(2,1)} reshape(bf16[3072,1536]{1,0:T(8,128)(2,1)} %convolution_convert_fusion.1) | data formatting | bytes 18874368 | tf_op jit(solution)/shard_map/convert_element_type | solution.py:156
  514.3 25.0 %copy.38 = bf16[1536,6448]{1,0:T(8,128)(2,1)} copy(bf16[1536,6448]{0,1:T(8,128)(2,1)} %convolution_convert_fusion) | data formatting | bytes 39616512 | tf_op jit(solution)/shard_map/convert_element_type | solution.py:156
  539.3 36.0 %convert_element_type.106 = bf16[9904128]{0:T(1024)(128)(2,1)} reshape(bf16[1536,6448]{1,0:T(8,128)(2,1)} %copy.38) | data formatting | bytes 39616512 | tf_op jit(solution)/shard_map/convert_element_type | solution.py:156
  575.4 16.7 %dynamic_update_slice.61 = bf16[14647296]{0:T(1024)(128)(2,1)} pad(bf16[9904128]{0:T(1024)(128)(2,1)} %convert_element_type.106, bf16[]{:T(256)} %constant.161.clone.1), padding=0_4743168 | pad | bytes 49102848 | tf_op jit(solution)/shard_map/dynamic_update_slice | solution.py:157
  592.1 8.7 constant_dynamic-update-slice_fusion.1
  611.7 3.3 fusion.74
  614.9 7.4 fusion.68
  622.3 430.1 %all-reduce.19.cloned.1.call-done = bf16[14647296]{0:T(1024)(128)(2,1)} async-done(((bf16[14647296]{0:T(1024)(128)(2,1)}), bf16[14647296]{0:T(1024)(128)(2,1)}) %all-reduce.19.cloned.1.call-update) | async-done | bytes 29294608 | tf_op jit(solution)/shard_map/psum | solution.py:159
  1052.5 90.0 %multiply_subtract_fusion = (f32[7323648]{0:T(1024)}, f32[7323648]{0:T(1024)}, f32[7323648]{0:T(1024)}) fusion(f32[7323648]{0:T(1024)} %param.15, f32[]{:T(128)} %bitcast.37, f32[]{:T(128)} %bitcast.36, f32[]{:T(128)} %bitcast.35, f32[]{:T(128)} %bitcast.34, f32[]{:T(128)} %bitcast.33, f32[]{:T(128)} %bitcast.32, f32[]{:T(128)} %bitcast.31, f32[]{:T(128)} %bitcast.30, ...), kind=kLoop, calls=%fused_computation.50 | loop fusion | flops 563920896 | bytes 190414928 | tf_op jit(solution)/shard_map/sub | solution.py:120
  (307 shorter events, 147.2 us)
Async XLA Ops:
  7.2 156.6 %all-gather.2.cloned.1.call-start = ((), (), s32[]{:S(2)}) async-start(), calls=%async_computation | async-start | bytes 15562752 | tf_op jit(solution)/shard_map/all_gather | solution.py:134
  7.2 41.8 %copy-start.10 = (bf16[256,1536]{1,0:T(8,128)(2,1)S(1)}, bf16[256,1536]{1,0:T(8,128)(2,1)}, u32[]{:S(2)}) copy-start(bf16[256,1536]{1,0:T(8,128)(2,1)} %param.12) | copy-start | bytes 2359300
  23.4 25.9 %copy-start.18 = (s32[256]{0:T(256)S(1)}, s32[256]{0:T(256)}, u32[]{:S(2)}) copy-start(s32[256]{0:T(256)} %param.14) | copy-start | bytes 3076
  24.7 23.3 %collective-permute-start = (bf16[457728]{0:T(1024)(128)(2,1)S(1)}, bf16[457728]{0:T(1024)(128)(2,1)S(1)}, u32[]{:S(2)}, u32[]{:S(2)}) collective-permute-start(bf16[457728]{0:T(1024)(128)(2,1)S(1)} %dynamic_slice.59), channel_id=1, source_target_pairs={{0,1},{1,0},{2,3},{3,2},{4,5},{5,4},{6,7},{7,6},{8,9},{9,8},{10,11... | collective-permute-start | bytes 2746376 | tf_op jit(solution)/shard_map/ppermute | solution.py:133
  49.0 1003.5 %all-reduce.19.cloned.1.call-start = ((), (), s32[]{:S(2)}) async-start(), calls=%async_computation.1 | async-start | bytes 58589184 | tf_op jit(solution)/shard_map/psum | solution.py:159
  49.3 139.5 %copy-start.33 = (f32[256]{0:T(256)}, f32[256]{0:T(256)S(1)}, u32[]{:S(2)}) copy-start(f32[256]{0:T(256)S(1)} %fusion.75) | copy-start | bytes 3076
  49.3 198.2 %copy-start.45 = (f32[256]{0:T(256)}, f32[256]{0:T(256)S(1)}, u32[]{:S(2)}) copy-start(f32[256]{0:T(256)S(1)} %fusion.99) | copy-start | bytes 3076
  49.4 211.4 %copy-start.35 = (pred[256]{0:T(512)(128)(4,1)}, pred[256]{0:T(512)(128)(4,1)S(1)}, u32[]{:S(2)}) copy-start(pred[256]{0:T(512)(128)(4,1)S(1)} %get-tuple-element.462) | copy-start | bytes 772
  49.4 211.4 %copy-start.37 = (pred[256]{0:T(512)(128)(4,1)}, pred[256]{0:T(512)(128)(4,1)S(1)}, u32[]{:S(2)}) copy-start(pred[256]{0:T(512)(128)(4,1)S(1)} %get-tuple-element.463) | copy-start | bytes 772
  49.4 211.4 %copy-start.39 = (pred[256]{0:T(512)(128)(4,1)}, pred[256]{0:T(512)(128)(4,1)S(1)}, u32[]{:S(2)}) copy-start(pred[256]{0:T(512)(128)(4,1)S(1)} %get-tuple-element.464) | copy-start | bytes 772
  194.4 66.4 %copy-start.21 = (f32[3328]{0:T(1024)}, f32[3328]{0:T(1024)S(1)}, u32[]{:S(2)}) copy-start(f32[3328]{0:T(1024)S(1)} %get-tuple-element.440) | copy-start | bytes 39940
  194.4 66.4 %copy-start.23 = (f32[3328]{0:T(1024)}, f32[3328]{0:T(1024)S(1)}, u32[]{:S(2)}) copy-start(f32[3328]{0:T(1024)S(1)} %get-tuple-element.441) | copy-start | bytes 39940
  194.4 66.4 %copy-start.25 = (f32[3328]{0:T(1024)}, f32[3328]{0:T(1024)S(1)}, u32[]{:S(2)}) copy-start(f32[3328]{0:T(1024)S(1)} %get-tuple-element.442) | copy-start | bytes 39940
  194.4 66.4 %copy-start.27 = (f32[3328]{0:T(1024)}, f32[3328]{0:T(1024)S(1)}, u32[]{:S(2)}) copy-start(f32[3328]{0:T(1024)S(1)} %get-tuple-element.443) | copy-start | bytes 39940
  260.5 20.3 %copy-start.7 = (f32[256,6448]{0,1:T(8,128)}, f32[256,6448]{0,1:T(8,128)S(1)}, u32[]{:S(2)}) copy-start(f32[256,6448]{0,1:T(8,128)S(1)} %fusion.80) | copy-start | bytes 19808260
  260.8 7.5 copy-start.3
  271.7 9.1 copy-start.42
  271.7 9.1 copy-start.48
  282.3 30.5 %copy-start.44 = (f32[48]{0:T(128)S(1)}, f32[48]{0:T(128)}, u32[]{:S(2)}) copy-start(f32[48]{0:T(128)} %get-tuple-element.430) | copy-start | bytes 580
  337.6 6.8 copy-start
  337.6 6.8 copy-start.12
  348.2 8.8 copy-start.9
  443.0 5.9 copy-start.15
  449.0 8.4 copy-start.22
  449.0 8.4 copy-start.24
  449.0 8.4 copy-start.26
  449.0 8.4 copy-start.28
  462.1 6.8 copy-start.46
  495.1 18.1 %copy-start.31 = (f32[3072]{0:T(1024)S(1)}, f32[3072]{0:T(1024)}, u32[]{:S(2)}) copy-start(f32[3072]{0:T(1024)} %get-tuple-element.413) | copy-start | bytes 36868
  495.1 19.0 %copy-start.30 = (f32[3328]{0:T(1024)S(1)}, f32[3328]{0:T(1024)}, u32[]{:S(2)}) copy-start(f32[3328]{0:T(1024)} %get-tuple-element.365) | copy-start | bytes 39940
  592.1 9.3 copy-start.32
  592.1 12.2 %copy-start.41 = (bf16[3072]{0:T(1024)(128)(2,1)S(1)}, bf16[3072]{0:T(1024)(128)(2,1)}, u32[]{:S(2)}) copy-start(bf16[3072]{0:T(1024)(128)(2,1)} %get-tuple-element.368) | copy-start | bytes 18436
  (32 other events, 132.9 us)
Sparse Core Ops, SparseCore 0:
  49.1 114.6 all-gather.1
  610.3 442.1 all-reduce.18
where the time goes:
time: 1160 us; the launch traced here: 1150 us
  waiting for transfers between devices  564 us (49%)
  other arithmetic  214 us (18%)
  local copies, waits for them, and re-layouts  206 us (18%)
  matrix products  146 us (13%)
  between operations  15.6 us (1%)
    psum x1, waiting for transfers between devices, reduce_gradient(): summed = lax.psum(flat_grad, ('rep', 'zero'))  430 us
    all_gather x1, waiting for transfers between devices, gather_weights(): other = lax.all_gather(other_piece, 'rep', axis=0, tiled=True)  114 us
    sub x1, other arithmetic, adamw(): return (new_first, new_second, weights - learn_rate * update)  90 us
    dot_general x36, matrix products, head_group(): return jnp.einsum('gts,gsp->gtp', kernel, group_values, precision=HIGHEST)  83.4 us
    convert_element_type x4, local copies, waits for them, and re-layouts, reduce_gradient(): flat_piece = piece_grad.reshape(-1).astype(jnp.bfloat16)  79.2 us
    dot_general x4, matrix products, contract(): lax.dot_general(left, right, (((left_dim,), (right_dim,)), ((), ())), pre...  36.8 us
    dynamic_update_slice x9, local copies, waits for them, and re-layouts, reduce_gradient(): lax.dynamic_update_slice_in_dim(flat_grad, flat_piece, offset, 0)  34.7 us
    reshape x1, local copies, waits for them, and re-layouts, unpack(): flat_values[bounds[piece_index]:bounds[piece_index + 1]]  32.9 us
  transfers between devices with their start and end apart: 3, of which 3 were waited for; matrix products, arithmetic and copies ran while one was open for 1% of the time, Pallas kernels for 0%

commit v1 on v0

--- a/solution.py
+++ b/solution.py
@@ -17,6 +17,29 @@
 BETA_TWO = 0.5
 HEAD_GROUP = 4
 HIGHEST = lax.Precision.HIGHEST
+
+
+def review_the_views(q_in, in_dim):
+    q_in = jnp.moveaxis(q_in, 0, in_dim)
+    opened = q_in.shape
+    return q_in.reshape(
+        *opened[:in_dim], opened[in_dim] * opened[in_dim + 1], *opened[in_dim + 2 :]
+    )
+
+
+def _enter_weights(mat, axis_key):
+    new = lax.axis_size(axis_key)
+    val, before = (new, lax.axis_index(axis_key))
+    newest, even = (mat[None], 1)
+    while even < val:
+        back = lax.ppermute(
+            newest, axis_name=axis_key, perm=tuple(((num, num ^ even) for num in range(val)))
+        )
+        row_out = before & even == 0
+        block_out = jnp.where(row_out, newest, back)
+        newest = jnp.concatenate([block_out, jnp.where(row_out, back, newest)])
+        even *= 2
+    return newest
 
 
 def piece_bounds():
@@ -131,7 +154,7 @@
     mine = lax.dynamic_slice_in_dim(own, rep_index * piece_size, piece_size)
     if zero_size == 2:
         other_piece = lax.ppermute(mine, "zero", [(0, 1), (1, 0)])
-        other = lax.all_gather(other_piece, "rep", axis=0, tiled=True)
+        other = review_the_views(_enter_weights(other_piece, "rep"), 0)
         shards = [jnp.where(zero_index == 0, own, other), jnp.where(zero_index == 0, other, own)]
     else:
         across = lax.all_gather(mine, "zero", axis=0, tiled=True)

time: 1160 us -> 1560 us (1.34)
  waiting for transfers between devices: 564 us -> 888 us
  other arithmetic: 214 us -> 263 us
  local copies, waits for them, and re-layouts: 206 us -> 225 us
    ppermute x0 -> x4, waiting for transfers between devices: none -> 436 us  [_enter_weights(): lax.ppermute(newest, axis_name=axis_key, perm=tuple(((num, num ^ even) fo...]
    all_gather x1 -> x0, waiting for transfers between devices: 114 us -> none  [gather_weights(): other = lax.all_gather(other_piece, 'rep', axis=0, tiled=True)]
    select_n x0 -> x4, other arithmetic: none -> 32.6 us  [_enter_weights(): block_out = jnp.where(row_out, newest, back)]
  transfers between devices with their start and end apart: 3 -> 6, of which waited for: 3 -> 6; matrix products, arithmetic and copies ran while one was open for 1% -> 1% of each run, Pallas kernels for 0% -> 0%
where the time goes in v1:
time: 1560 us; the launch traced here: 1550 us
  waiting for transfers between devices  888 us (57%)
  other arithmetic  263 us (17%)
  local copies, waits for them, and re-layouts  225 us (14%)
  matrix products  147 us (9%)
  between operations  15.9 us (1%)
    ppermute x4, waiting for transfers between devices, _enter_weights(): lax.ppermute(newest, axis_name=axis_key, perm=tuple(((num, num ^ even) fo...  436 us
    psum x1, waiting for transfers between devices, reduce_gradient(): summed = lax.psum(flat_grad, ('rep', 'zero'))  432 us
    sub x1, other arithmetic, adamw(): return (new_first, new_second, weights - learn_rate * update)  90.1 us
    dot_general x36, matrix products, head_group(): return jnp.einsum('gts,gsp->gtp', kernel, group_values, precision=HIGHEST)  83.4 us
    convert_element_type x4, local copies, waits for them, and re-layouts, reduce_gradient(): flat_piece = piece_grad.reshape(-1).astype(jnp.bfloat16)  79.2 us
    dot_general x4, matrix products, contract(): lax.dot_general(left, right, (((left_dim,), (right_dim,)), ((), ())), pre...  36.6 us
    dynamic_update_slice x9, local copies, waits for them, and re-layouts, reduce_gradient(): lax.dynamic_update_slice_in_dim(flat_grad, flat_piece, offset, 0)  34.8 us
    reshape x1, local copies, waits for them, and re-layouts, unpack(): flat_values[bounds[piece_index]:bounds[piece_index + 1]]  32.9 us
  transfers between devices with their start and end apart: 6, of which 6 were waited for; matrix products, arithmetic and copies ran while one was open for 1% of the time, Pallas kernels for 0%

profile of v1, /device:TPU:0, one launch (start us, length us, event | category | flops | bytes accessed | tf_op | source)
XLA Modules:
  0.0 1548.4 jit_solution(8972436671228793265)
XLA Ops:
  7.2 16.1 %convert_element_type.91 = bf16[7323648]{0:T(1024)(128)(2,1)} convert(f32[7323648]{0:T(1024)} %param.15) | non-fusion elementwise | flops 7323648 | bytes 43941888 | tf_op jit(solution)/shard_map/convert_element_type | solution.py:153
  27.6 20.3 %collective-permute-done = bf16[457728]{0:T(1024)(128)(2,1)S(1)} collective-permute-done((bf16[457728]{0:T(1024)(128)(2,1)S(1)}, bf16[457728]{0:T(1024)(128)(2,1)S(1)}, u32[]{:S(2)}, u32[]{:S(2)}) %collective-permute-start) | collective-permute-done | bytes 915488 | tf_op jit(solution)/shard_map/ppermute | solution.py:156
  47.9 11.2 broadcast_in_dim.226
  63.1 10.4 broadcast_select_fusion.5
  80.8 40.3 %collective-permute-done.2 = bf16[2,457728]{1,0:T(2,128)(2,1)} collective-permute-done((bf16[2,457728]{1,0:T(2,128)(2,1)S(1)}, bf16[2,457728]{1,0:T(2,128)(2,1)}, u32[]{:S(2)}, u32[]{:S(2)}) %collective-permute-start.2) | collective-permute-done | bytes 1830944 | tf_op jit(solution)/shard_map/ppermute | solution.py:35
  121.1 7.0 broadcast_select_fusion.7
  134.7 78.9 %collective-permute-done.3 = bf16[4,457728]{1,0:T(4,128)(2,1)} collective-permute-done((bf16[4,457728]{1,0:T(4,128)(2,1)}, bf16[4,457728]{1,0:T(4,128)(2,1)}, u32[]{:S(2)}, u32[]{:S(2)}) %collective-permute-start.3) | collective-permute-done | bytes 3661856 | tf_op jit(solution)/shard_map/ppermute | solution.py:35
  213.7 7.1 broadcast_select_fusion.9
  230.6 312.4 %collective-permute-done.4 = bf16[8,457728]{1,0:T(8,128)(2,1)} collective-permute-done((bf16[8,457728]{1,0:T(8,128)(2,1)}, bf16[8,457728]{1,0:T(8,128)(2,1)}, u32[]{:S(2)}, u32[]{:S(2)}) %collective-permute-start.4) | collective-permute-done | bytes 7323680 | tf_op jit(solution)/shard_map/ppermute | solution.py:35
  543.0 8.1 broadcast_select_fusion.3
  552.2 7.1 copy.36
  559.3 25.1 %broadcast_select_fusion = (bf16[7323648]{0:T(1024)(128)(2,1)}, bf16[7323648]{0:T(1024)(128)(2,1)}) fusion(bf16[7323648]{0:T(1024)(128)(2,1)} %bitcast.152, pred[]{:T(512)S(6)} %eq.51, f32[7323648]{0:T(1024)} %param.15), kind=kLoop, calls=%fused_computation.82 | loop fusion | flops 21970944 | bytes 73236480 | tf_op jit(solution)/shard_map/jit(_where)/select_n | solution.py:158
  589.9 20.2 %pad_maximum_fusion = bf16[9904128]{0:T(1024)(128)(2,1)} fusion(bf16[7323648]{0:T(1024)(128)(2,1)} %get-tuple-element.429, bf16[7323648]{0:T(1024)(128)(2,1)} %get-tuple-element.428), kind=kLoop, calls=%fused_computation.80 | loop fusion | flops 39616512 | bytes 49102848 | tf_op jit(solution)/shard_map/concatenate | solution.py:170
  610.1 32.9 %reshape.264 = bf16[1536,6448]{1,0:T(8,128)(2,1)} reshape(bf16[9904128]{0:T(1024)(128)(2,1)} %pad_maximum_fusion) | data formatting | bytes 39616512 | tf_op jit(solution)/shard_map/reshape | solution.py:58
  643.0 13.0 fusion.80
  656.3 7.8 fusion.64
  667.6 9.1 slice.224
  678.2 30.3 %while.33 = (s32[]{:T(128)}, f32[12,4,256,64]{2,3,1,0:T(8,128)S(1)}, f32[12,4,256]{2,1,0:T(4,128)S(1)}, f32[1,256,256]{2,1,0:T(8,128)}, f32[12,4,256]{2,1,0:T(4,...) while((s32[]{:T(128)}, f32[12,4,256,64]{2,3,1,0:T(8,128)S(1)}, ...), condition=%wide.region_4.5_spmd.clone, body=%wide.region_3.4_spmd.clone.sunk | while | flops 202375168 | bytes 881761 | solution.py:113
  715.4 17.9 %slice.185 = bf16[3072,1536]{1,0:T(8,128)(2,1)} reshape(bf16[4718592]{0:T(1024)(128)(2,1)} %slice.224) | data formatting | bytes 18874368 | tf_op jit(solution)/shard_map/slice | solution.py:58
  752.7 78.2 %while.34 = (s32[]{:T(128)}, f32[256,256]{1,0:T(8,128)S(1)}, f32[12,4,256]{2,1,0:T(4,128)S(1)}, f32[12,4,256]{2,1,0:T(4,128)S(1)}, f32[12,4,256,64]{2,3,1,0:T(8,...) while((s32[]{:T(128)}, f32[256,256]{1,0:T(8,128)S(1)}, ...), condition=%wide.region_12.13_spmd.clone, body=%wide.region_7.12_spmd.clone.sunk | while | flops 407370752 | bytes 4986067 | solution.py:113
  844.7 8.4 multiply_reduce_fusion.4
  857.8 6.8 pad_add_fusion
  864.6 12.9 fusion.72
  877.5 13.1 convolution_convert_fusion
  890.6 18.1 %convert_element_type.108 = bf16[4718592]{0:T(1024)(128)(2,1)} reshape(bf16[3072,1536]{1,0:T(8,128)(2,1)} %convolution_convert_fusion.1) | data formatting | bytes 18874368 | tf_op jit(solution)/shard_map/convert_element_type | solution.py:179
  909.7 25.0 %copy.31 = bf16[1536,6448]{1,0:T(8,128)(2,1)} copy(bf16[1536,6448]{0,1:T(8,128)(2,1)} %convolution_convert_fusion) | data formatting | bytes 39616512 | tf_op jit(solution)/shard_map/convert_element_type | solution.py:179
  934.8 36.0 %convert_element_type.106 = bf16[9904128]{0:T(1024)(128)(2,1)} reshape(bf16[1536,6448]{1,0:T(8,128)(2,1)} %copy.31) | data formatting | bytes 39616512 | tf_op jit(solution)/shard_map/convert_element_type | solution.py:179
  970.9 16.7 %dynamic_update_slice.61 = bf16[14647296]{0:T(1024)(128)(2,1)} pad(bf16[9904128]{0:T(1024)(128)(2,1)} %convert_element_type.106, bf16[]{:T(256)} %constant.169.clone.1), padding=0_4743168 | pad | bytes 49102848 | tf_op jit(solution)/shard_map/dynamic_update_slice | solution.py:180
  987.6 8.7 constant_dynamic-update-slice_fusion.1
  1010.5 8.6 fusion.68
  1019.1 431.9 %all-reduce.19.cloned.1.call-done = bf16[14647296]{0:T(1024)(128)(2,1)} async-done(((bf16[14647296]{0:T(1024)(128)(2,1)}), bf16[14647296]{0:T(1024)(128)(2,1)}) %all-reduce.19.cloned.1.call-update) | async-done | bytes 29294608 | tf_op jit(solution)/shard_map/psum | solution.py:182
  1451.0 90.1 %multiply_subtract_fusion = (f32[7323648]{0:T(1024)}, f32[7323648]{0:T(1024)}, f32[7323648]{0:T(1024)}) fusion(f32[7323648]{0:T(1024)} %param.15, f32[]{:T(128)} %bitcast.37, f32[]{:T(128)} %bitcast.36, f32[]{:T(128)} %bitcast.35, f32[]{:T(128)} %bitcast.34, f32[]{:T(128)} %bitcast.33, f32[]{:T(128)} %bitcast.32, f32[]{:T(128)} %bitcast.31, f32[]{:T(128)} %bitcast.30, ...), kind=kLoop, calls=%fused_computation.50 | loop fusion | flops 563920896 | bytes 190414928 | tf_op jit(solution)/shard_map/sub | solution.py:143
  (330 shorter events, 210.3 us)
Async XLA Ops:
  7.2 1443.8 %all-reduce.19.cloned.1.call-start = ((), (), s32[]{:S(2)}) async-start(), calls=%async_computation | async-start | bytes 58589184 | tf_op jit(solution)/shard_map/psum | solution.py:182
  24.6 23.3 %collective-permute-start = (bf16[457728]{0:T(1024)(128)(2,1)S(1)}, bf16[457728]{0:T(1024)(128)(2,1)S(1)}, u32[]{:S(2)}, u32[]{:S(2)}) collective-permute-start(bf16[457728]{0:T(1024)(128)(2,1)S(1)} %dynamic_slice.59), channel_id=1, source_target_pairs={{0,1},{1,0},{2,3},{3,2},{4,5},{5,4},{6,7},{7,6},{8,9},{9,8},{10,11... | collective-permute-start | bytes 2746376 | tf_op jit(solution)/shard_map/ppermute | solution.py:156
  59.1 4.0 collective-permute-start.1
  78.9 42.2 %collective-permute-start.2 = (bf16[2,457728]{1,0:T(2,128)(2,1)S(1)}, bf16[2,457728]{1,0:T(2,128)(2,1)}, u32[]{:S(2)}, u32[]{:S(2)}) collective-permute-start(bf16[2,457728]{1,0:T(2,128)(2,1)S(1)} %pad_maximum_fusion.3), channel_id=1, source_target_pairs={{0,4},{2,6},{4,0},{6,2},{8,12},{10,14},{12,8},{14,10},{16,20},{18,... | collective-permute-start | bytes 5492744 | tf_op jit(solution)/shard_map/ppermute | solution.py:35
  132.9 80.7 %collective-permute-start.3 = (bf16[4,457728]{1,0:T(4,128)(2,1)}, bf16[4,457728]{1,0:T(4,128)(2,1)}, u32[]{:S(2)}, u32[]{:S(2)}) collective-permute-start(bf16[4,457728]{1,0:T(4,128)(2,1)} %pad_maximum_fusion.2), channel_id=1, source_target_pairs={{0,8},{2,10},{4,12},{6,14},{8,0},{10,2},{12,4},{14,6},{16,24},{18,... | collective-permute-start | bytes 10985480 | tf_op jit(solution)/shard_map/ppermute | solution.py:35
  220.7 8.7 copy-start.15
  220.8 9.0 copy-start.22
  226.7 316.2 %collective-permute-start.4 = (bf16[8,457728]{1,0:T(8,128)(2,1)}, bf16[8,457728]{1,0:T(8,128)(2,1)}, u32[]{:S(2)}, u32[]{:S(2)}) collective-permute-start(bf16[8,457728]{1,0:T(8,128)(2,1)} %pad_maximum_fusion.1), channel_id=1, source_target_pairs={{0,16},{2,18},{4,20},{6,22},{8,24},{10,26},{12,28},{14,30},{16,0},... | collective-permute-start | bytes 21970952 | tf_op jit(solution)/shard_map/ppermute | solution.py:35
  229.7 321.4 %copy-start.37 = (f32[256]{0:T(256)}, f32[256]{0:T(256)S(1)}, u32[]{:S(2)}) copy-start(f32[256]{0:T(256)S(1)} %fusion.75) | copy-start | bytes 3076
  229.8 413.2 %copy-start.49 = (f32[256]{0:T(256)}, f32[256]{0:T(256)S(1)}, u32[]{:S(2)}) copy-start(f32[256]{0:T(256)S(1)} %fusion.99) | copy-start | bytes 3076
  229.8 426.4 %copy-start.39 = (pred[256]{0:T(512)(128)(4,1)}, pred[256]{0:T(512)(128)(4,1)S(1)}, u32[]{:S(2)}) copy-start(pred[256]{0:T(512)(128)(4,1)S(1)} %get-tuple-element.470) | copy-start | bytes 772
  229.8 426.4 %copy-start.41 = (pred[256]{0:T(512)(128)(4,1)}, pred[256]{0:T(512)(128)(4,1)S(1)}, u32[]{:S(2)}) copy-start(pred[256]{0:T(512)(128)(4,1)S(1)} %get-tuple-element.471) | copy-start | bytes 772
  229.8 426.4 %copy-start.43 = (pred[256]{0:T(512)(128)(4,1)}, pred[256]{0:T(512)(128)(4,1)S(1)}, u32[]{:S(2)}) copy-start(pred[256]{0:T(512)(128)(4,1)S(1)} %get-tuple-element.472) | copy-start | bytes 772
  589.9 66.4 %copy-start.25 = (f32[3328]{0:T(1024)}, f32[3328]{0:T(1024)S(1)}, u32[]{:S(2)}) copy-start(f32[3328]{0:T(1024)S(1)} %get-tuple-element.448) | copy-start | bytes 39940
  589.9 66.4 %copy-start.27 = (f32[3328]{0:T(1024)}, f32[3328]{0:T(1024)S(1)}, u32[]{:S(2)}) copy-start(f32[3328]{0:T(1024)S(1)} %get-tuple-element.449) | copy-start | bytes 39940
  589.9 66.4 %copy-start.29 = (f32[3328]{0:T(1024)}, f32[3328]{0:T(1024)S(1)}, u32[]{:S(2)}) copy-start(f32[3328]{0:T(1024)S(1)} %get-tuple-element.450) | copy-start | bytes 39940
  589.9 66.4 %copy-start.31 = (f32[3328]{0:T(1024)}, f32[3328]{0:T(1024)S(1)}, u32[]{:S(2)}) copy-start(f32[3328]{0:T(1024)S(1)} %get-tuple-element.451) | copy-start | bytes 39940
  656.0 20.7 %copy-start.9 = (f32[256,6448]{0,1:T(8,128)}, f32[256,6448]{0,1:T(8,128)S(1)}, u32[]{:S(2)}) copy-start(f32[256,6448]{0,1:T(8,128)S(1)} %fusion.80) | copy-start | bytes 19808260
  656.3 7.9 copy-start.5
  667.6 9.1 copy-start.46
  667.6 9.1 copy-start.52
  678.2 30.3 %copy-start.48 = (f32[48]{0:T(128)S(1)}, f32[48]{0:T(128)}, u32[]{:S(2)}) copy-start(f32[48]{0:T(128)} %get-tuple-element.430) | copy-start | bytes 580
  744.0 8.8 copy-start.14
  844.7 8.4 copy-start.26
  844.7 8.4 copy-start.28
  844.7 8.4 copy-start.30
  844.7 8.4 copy-start.32
  857.8 6.8 copy-start.50
  890.6 18.1 %copy-start.35 = (f32[3072]{0:T(1024)S(1)}, f32[3072]{0:T(1024)}, u32[]{:S(2)}) copy-start(f32[3072]{0:T(1024)} %get-tuple-element.413) | copy-start | bytes 36868
  890.6 19.0 %copy-start.34 = (f32[3328]{0:T(1024)S(1)}, f32[3328]{0:T(1024)}, u32[]{:S(2)}) copy-start(f32[3328]{0:T(1024)} %get-tuple-element.365) | copy-start | bytes 39940
  987.5 9.3 copy-start.36
  987.5 12.2 copy-start.45
  (39 other events, 174.9 us)
Sparse Core Ops, SparseCore 0:
  1005.9 445.0 all-reduce.18
